TPU v7x, 32 devices: a whole 2x2x4 slice. The times are simulated.
32 devices in a mesh: slab: 8 (over y, x, core), pencil: 4 (over z).
Axes of the slice: x: 2, y: 2, z: 4, core: 2. Of those that a mesh axis runs over, the one named last changes fastest.
Arguments:
- descriptors: bfloat16 [49152, 1600], P(('slab', 'pencil')), may hold values from -6 to 6
- species: int32 [49152], P(('slab', 'pencil')), may hold values from 0 to 3
- bucket_count: int32 [128], P(('slab', 'pencil')), may hold values from 288 to 384, as said below
- base_index: int32 [3, 49152], P(None, ('slab', 'pencil')), may hold values from 0 to 383, as said below
- fraction: float32 [3, 49152], P(None, ('slab', 'pencil')), may hold values from 0 to 0.999
- weight_in: bfloat16 [1600, 256], replicated, may hold values from -0.15625 to 0.15625
- bias_in: float32 [256], replicated, may hold values from -4 to 4
- weight_mid: bfloat16 [2, 256, 256], replicated, may hold values from -0.375 to 0.375
- bias_mid: float32 [2, 256], replicated, may hold values from -4 to 4
- weight_out: bfloat16 [3, 256], replicated, may hold values from -0.0390625 to 0.0390625
- bias_out: float32 [3], replicated, may hold values from -0.2 to 0.2
Outputs:
- energy: float32 [], replicated
- site_forces: float32 [2, 3, 49152], P(None, None, ('slab', 'pencil'))
- descriptor_grad: bfloat16 [49152, 1600], P(('slab', 'pencil'))
Inputs may be any that keep to these rules, and one draw needn't show every extreme that they name: Slot i is in use when i % 384 < bucket_count[i // 384]. Among the buckets of every device at least one is full. Slots come in blocks of 1536; block d belongs to slab index d // 4 and pencil index d % 4. base_index[0, i] lies in that slab's planes, within the 4 planes of the slot's bucket (bucket b covers that slab's planes (b % 4) * 4 onwards); base_index[1, i] lies in that pencil's 48 rows; base_index[2, i] is any column.
All inputs are finite; a program needn't handle non-finite values.
Results may differ from a plain program's by a relative error of at most 0.018.
Values sent between devices are 32-bit elements; how exact they have to be, the bound alone decides.
No kernel may reach another device: no remote copies, remote signals or barrier semaphores. Data moves between devices by JAX's collectives and lax.ppermute only.
A program may use at most 192 MiB of HBM per device.

v0:
```python
import math
import jax
import jax.numpy as jnp
from jax import lax
from jax.sharding import PartitionSpec as P

NX = 384
CZ = 16
CY = 48
BZ = 4
ion_table = (6.0, 1.0, 9.0, 7.0)
wannier_table = (-8.0, 0.0, -8.0, -8.0)
spline_coeffs = (1.0 / 120.0, 26.0 / 120.0, 66.0 / 120.0, 26.0 / 120.0, 1.0 / 120.0)
ewald_beta = 1.4
shift_scale = 0.9
highest = lax.Precision.HIGHEST


def extended(cells, sides, width):
    for axis, dim in sides:
        count = lax.axis_size(axis)
        head = lax.slice_in_dim(cells, 0, width, axis=dim)
        tail = lax.slice_in_dim(cells, cells.shape[dim] - width, cells.shape[dim], axis=dim)
        cells = jnp.concatenate(
            [
                lax.ppermute(tail, axis, [(i, (i + 1) % count) for i in range(count)]),
                cells,
                lax.ppermute(head, axis, [((i + 1) % count, i) for i in range(count)]),
            ],
            axis=dim,
        )
    return cells


def bspline(offset):
    folded = jnp.minimum(offset, 6.0 - offset)
    part_one = jnp.maximum(folded, 0.0)
    part_two = jnp.maximum(folded - 1.0, 0.0)
    part_three = jnp.maximum(folded - 2.0, 0.0)
    spline_val = (part_one**5 - 6.0 * part_two**5 + 15.0 * part_three**5) / 120.0
    spline_slope = (part_one**4 - 6.0 * part_two**4 + 15.0 * part_three**4) / 24.0
    return (spline_val, jnp.where(offset <= 3.0, spline_slope, -spline_slope))


def species_charge(species, charge_list):
    kind_ids = jnp.arange(len(charge_list), dtype=jnp.int32)
    levels = jnp.asarray(charge_list, jnp.float32)
    picked = jnp.where(species[None, :] == kind_ids[:, None], levels[:, None], 0.0)
    return jnp.sum(picked, axis=0)


def fitting(descriptors, weight_in, bias_in, weight_mid, bias_mid, weight_out, bias_out):
    hidden = jnp.tanh(
        jnp.dot(descriptors, weight_in, preferred_element_type=jnp.float32) + bias_in
    ).astype(jnp.bfloat16)
    for layer_idx in range(weight_mid.shape[0]):
        pre_act = (
            jnp.dot(hidden, weight_mid[layer_idx], preferred_element_type=jnp.float32)
            + bias_mid[layer_idx]
        )
        hidden = (hidden.astype(jnp.float32) + jnp.tanh(pre_act)).astype(jnp.bfloat16)
    output_raw = lax.dot_general(
        weight_out, hidden, (((1,), (1,)), ((), ())), preferred_element_type=jnp.float32
    )
    return shift_scale * jnp.tanh(output_raw + bias_out[:, None])


def axis_terms(index, length):
    signed = jnp.where(2 * index >= length, index - length, index).astype(jnp.float32) / length
    orders = jnp.arange(1, 6, dtype=jnp.int32)
    phases = (index[:, None] * orders[None, :] % length).astype(jnp.float32) * (
        2.0 * math.pi / length
    )
    coeffs = jnp.asarray(spline_coeffs, jnp.float32)
    real_sum = jnp.sum(coeffs[None, :] * jnp.cos(phases), axis=1)
    imag_sum = jnp.sum(coeffs[None, :] * jnp.sin(phases), axis=1)
    modulus = 1.0 / (real_sum * real_sum + imag_sum * imag_sum)
    damping = jnp.exp(-((math.pi / ewald_beta) ** 2) * signed * signed)
    return (signed * signed, damping * modulus)


def influence(z_index, z_len, y_index, y_len, x_index, x_len):
    z_sq, z_fac = axis_terms(z_index, z_len)
    y_sq, y_fac = axis_terms(y_index, y_len)
    x_sq, x_fac = axis_terms(x_index, x_len)
    squared = z_sq[:, None, None] + y_sq[None, :, None] + x_sq[None, None, :]
    safe_sq = jnp.where(squared > 0.0, squared, 1.0)
    volume = float(z_len * y_len * x_len)
    scaled = (
        z_fac[:, None, None]
        * y_fac[None, :, None]
        * x_fac[None, None, :]
        / (math.pi * volume * safe_sq)
    )
    return jnp.where(squared > 0.0, scaled, 0.0)


def dft_table(length):
    index = jnp.arange(length, dtype=jnp.int32)
    angles = (index[:, None] * index[None, :] % length).astype(jnp.float32) * (
        2.0 * math.pi / length
    )
    return (jnp.cos(angles), jnp.sin(angles))


def half_table(length, width):
    positions = jnp.arange(length, dtype=jnp.int32)
    wave_ids = jnp.arange(width, dtype=jnp.int32)
    angles = (positions[:, None] * wave_ids[None, :] % length).astype(jnp.float32) * (
        2.0 * math.pi / length
    )
    kept_mask = (2 * wave_ids <= length).astype(jnp.float32)
    doubled = (
        jnp.where((wave_ids == 0) | (2 * wave_ids == length), 1.0, 2.0).astype(jnp.float32)
        * kept_mask
    )
    return (jnp.cos(angles) * kept_mask[None, :], jnp.sin(angles) * kept_mask[None, :], doubled)


def dense_window(relative, start, length):
    steps_idx = jnp.arange(8, dtype=jnp.int32)
    spline_val, spline_slope = bspline(
        relative[:, None] - steps_idx.astype(jnp.float32)[None, :] + 6.0
    )
    cell_ids = jnp.arange(length, dtype=jnp.int32)
    target = (start[:, None] + steps_idx[None, :]) % length
    matches = target[:, :, None] == cell_ids[None, None, :]
    dense_val = jnp.sum(jnp.where(matches, spline_val[:, :, None], 0.0), axis=1)
    dense_slope = jnp.sum(jnp.where(matches, spline_slope[:, :, None], 0.0), axis=1)
    return (dense_val, dense_slope)


def lead_product(table, data, dim):
    return lax.dot_general(table, data, (((1,), (dim,)), ((), ())), precision=highest)


def forward_pair(cosine, sine, real_part, imag_part, dim):
    real_cos = lead_product(cosine, real_part, dim)
    imag_sin = lead_product(sine, imag_part, dim)
    imag_cos = lead_product(cosine, imag_part, dim)
    real_sin = lead_product(sine, real_part, dim)
    return (real_cos + imag_sin, imag_cos - real_sin)


def inverse_pair(cosine, sine, real_part, imag_part, dim):
    real_cos = lead_product(cosine, real_part, dim)
    imag_sin = lead_product(sine, imag_part, dim)
    imag_cos = lead_product(cosine, imag_part, dim)
    real_sin = lead_product(sine, real_part, dim)
    return (real_cos - imag_sin, real_sin + imag_cos)


def body(
    descriptors,
    species,
    bucket_count,
    base_index,
    fraction,
    weight_in,
    bias_in,
    weight_mid,
    bias_mid,
    weight_out,
    bias_out,
):
    n_slab = lax.axis_size("slab")
    n_pencil = lax.axis_size("pencil")
    slab_idx = lax.axis_index("slab")
    pencil_idx = lax.axis_index("pencil")
    rows_all = CY * n_pencil
    planes_all = CZ * n_slab
    row_part = rows_all // n_slab
    half_cols = NX // 2 + 1
    wave_cols = -(-half_cols // n_pencil) * n_pencil
    column_part = wave_cols // n_pencil
    n_buckets = bucket_count.shape[0]
    capacity = species.shape[0] // n_buckets
    site_count = 2 * capacity
    slot_ids = jnp.arange(capacity, dtype=jnp.int32)
    in_use = (slot_ids[None, :] < bucket_count[:, None]).reshape(-1).astype(jnp.float32)
    charges = (
        jnp.stack([species_charge(species, ion_table), species_charge(species, wannier_table)])
        * in_use[None, :]
    )

    def network(features):
        return fitting(features, weight_in, bias_in, weight_mid, bias_mid, weight_out, bias_out)

    centroid_shift, pullback = jax.vjp(network, descriptors)
    relative = jnp.stack([fraction, fraction + centroid_shift])
    anchor = jnp.stack([slab_idx * CZ, pencil_idx * CY, jnp.zeros((), jnp.int32)])
    local_base = base_index - anchor[:, None]
    site_charge = (
        charges.reshape(2, n_buckets, capacity).transpose(1, 0, 2).reshape(n_buckets, site_count)
    )
    site_rel = (
        relative.reshape(2, 3, n_buckets, capacity)
        .transpose(2, 1, 0, 3)
        .reshape(n_buckets, 3, site_count)
    )
    site_base = jnp.broadcast_to(
        local_base.reshape(3, n_buckets, 1, capacity), (3, n_buckets, 2, capacity)
    )
    site_base = site_base.transpose(1, 0, 2, 3).reshape(n_buckets, 3, site_count)
    bucket_ids = jnp.arange(n_buckets, dtype=jnp.int32)
    window_shape = (BZ + 8, CY + 8, NX)
    zero_index = jnp.zeros((), jnp.int32)

    def spread_step(grid_now, inputs):
        bucket, charge, rel_pos, base_pos = inputs
        plane_val, plane_slope = dense_window(rel_pos[0], base_pos[0] - bucket * BZ + 1, BZ + 8)
        row_val, row_slope = dense_window(rel_pos[1], base_pos[1] + 1, CY + 8)
        col_val, col_slope = dense_window(rel_pos[2], base_pos[2] - 3, NX)
        outer_prod = ((charge[:, None] * plane_val)[:, :, None] * row_val[:, None, :]).reshape(
            site_count, -1
        )
        block_sum = lax.dot_general(
            outer_prod, col_val, (((0,), (0,)), ((), ())), precision=highest
        )
        corner = (bucket * BZ, zero_index, zero_index)
        current = lax.dynamic_slice(grid_now, corner, window_shape)
        grid_now = lax.dynamic_update_slice(
            grid_now, current + block_sum.reshape(window_shape), corner
        )
        return (grid_now, (plane_val, plane_slope, row_val, row_slope, col_val, col_slope))

    charge_grid, windows = lax.scan(
        spread_step,
        jnp.zeros((CZ + 8, CY + 8, NX), jnp.float32),
        (bucket_ids, site_charge, site_rel, site_base),
    )
    half_cos, half_sin, doubled = half_table(NX, wave_cols)
    forward_rows = jnp.stack([half_cos.T, -half_sin.T], axis=1).reshape(2 * wave_cols, NX)
    inverse_rows = jnp.stack(
        [(half_cos * doubled[None, :]).T, (-half_sin * doubled[None, :]).T], axis=0
    )
    row_cos, row_sin = dft_table(rows_all)
    plane_cos, plane_sin = dft_table(planes_all)
    rim_planes = jnp.concatenate([charge_grid[:4], charge_grid[CZ + 4 :]], axis=0)
    arrived = extended(rim_planes, (("slab", 0),), 4)
    inner_grid = charge_grid[4 : CZ + 4].at[:4].add(arrived[:4]).at[CZ - 4 :].add(arrived[12:])
    rim_rows = jnp.concatenate([inner_grid[:, :4], inner_grid[:, CY + 4 :]], axis=1)
    arrived = extended(rim_rows, (("pencil", 1),), 4)
    source_grid = (
        inner_grid[:, 4 : CY + 4].at[:, :4].add(arrived[:, :4]).at[:, CY - 4 :].add(arrived[:, 12:])
    )
    plane_here = source_grid.shape[0]
    row_here = source_grid.shape[1]
    spectrum = lead_product(forward_rows, source_grid, 2).reshape(
        wave_cols, 2, plane_here, row_here
    )
    spectrum = lax.all_to_all(spectrum, "pencil", split_axis=0, concat_axis=3, tiled=True)
    real_y, imag_y = forward_pair(row_cos, row_sin, spectrum[:, 0], spectrum[:, 1], 2)
    spectrum = jnp.stack([real_y, imag_y], axis=1)
    spectrum = lax.all_to_all(spectrum, "slab", split_axis=0, concat_axis=3, tiled=True)
    real_z, imag_z = forward_pair(plane_cos, plane_sin, spectrum[:, 0], spectrum[:, 1], 2)
    x_ids = pencil_idx * column_part + jnp.arange(column_part, dtype=jnp.int32)
    factor = influence(
        jnp.arange(planes_all, dtype=jnp.int32),
        planes_all,
        slab_idx * row_part + jnp.arange(row_part, dtype=jnp.int32),
        rows_all,
        x_ids,
        NX,
    )
    weighted_real = real_z * factor
    weighted_imag = imag_z * factor
    power = weighted_real * real_z + weighted_imag * imag_z
    x_weight = jnp.where((x_ids == 0) | (2 * x_ids == NX), 1.0, 2.0).astype(jnp.float32)
    x_weight = x_weight * (2 * x_ids <= NX).astype(jnp.float32)
    energy_terms = 0.5 * jnp.sum(power * x_weight)
    energy_sum = lax.psum(energy_terms, ("slab", "pencil"))
    back_real, back_imag = inverse_pair(plane_cos, plane_sin, weighted_real, weighted_imag, 0)
    returned = jnp.stack([back_real, back_imag], axis=1)
    returned = lax.all_to_all(returned, "slab", split_axis=0, concat_axis=2, tiled=True)
    back_real, back_imag = inverse_pair(row_cos, row_sin, returned[:, 0], returned[:, 1], 1)
    returned = jnp.stack([back_real, back_imag], axis=1)
    returned = lax.all_to_all(returned, "pencil", split_axis=0, concat_axis=3, tiled=True)
    potential = lax.dot_general(
        returned, inverse_rows, (((1, 3), (0, 1)), ((), ())), precision=highest
    )
    potential = extended(potential, (("slab", 1), ("pencil", 0)), 4)

    def sample_step(inputs):
        bucket, plane_val, plane_slope, row_val, row_slope, col_val, col_slope = inputs
        corner = (zero_index, bucket * BZ, zero_index)
        patch = lax.dynamic_slice(potential, corner, (CY + 8, BZ + 8, NX)).reshape(-1, NX)
        stacked = jnp.concatenate([col_val, col_slope], axis=0)
        both = lax.dot_general(stacked, patch, (((1,), (1,)), ((), ())), precision=highest)
        along = both[:site_count].reshape(site_count, CY + 8, BZ + 8)
        across = both[site_count:].reshape(site_count, CY + 8, BZ + 8)
        site_level = jnp.einsum("sz,sy,syz->s", plane_val, row_val, along, precision=highest)
        grad_z = jnp.einsum("sz,sy,syz->s", plane_slope, row_val, along, precision=highest)
        grad_y = jnp.einsum("sz,sy,syz->s", plane_val, row_slope, along, precision=highest)
        grad_x = jnp.einsum("sz,sy,syz->s", plane_val, row_val, across, precision=highest)
        return (site_level, jnp.stack([grad_z, grad_y, grad_x]))

    levels, slopes = lax.map(sample_step, (bucket_ids,) + tuple(windows))
    forces = -site_charge[:, None, :] * slopes
    site_forces = forces.reshape(n_buckets, 3, 2, capacity).transpose(2, 1, 0, 3).reshape(2, 3, -1)
    (descriptor_grad,) = pullback(-site_forces[1])
    total_slots = species.shape[0] * n_slab * n_pencil
    energy = energy_sum / float(total_slots)
    return (energy, site_forces, descriptor_grad)


def solution(mesh):
    in_specs = (
        P(("slab", "pencil"), None),
        P(("slab", "pencil")),
        P(("slab", "pencil")),
        P(None, ("slab", "pencil")),
        P(None, ("slab", "pencil")),
        P(),
        P(),
        P(),
        P(),
        P(),
        P(),
    )
    out_specs = (P(), P(None, None, ("slab", "pencil")), P(("slab", "pencil"), None))
    return jax.shard_map(body, mesh=mesh, in_specs=in_specs, out_specs=out_specs, check_vma=False)
```

profile of v0, /device:TPU:12, one launch (start us, length us, event | category | flops | bytes accessed | tf_op | source)
XLA Modules:
  0.0 749.2 jit_solution(451744507878971859)
XLA Ops:
  13.4 99.9 %while.39 = (s32[]{:T(128)}, f32[24,56,384]{2,1,0:T(8,128)}, f32[4,768,12]{1,2,0:T(8,128)S(1)}, f32[4,768,12]{1,2,0:T(8,128)}, f32[4,768,56]{1,2,0:T(8,128)}, /*...) while((s32[]{:T(128)}, f32[24,56,384]{2,1,0:T(8,128)}, ...), condition=%wide.region_9.10_spmd, body=%wide.region_2.9_spmd.sunk | while | flops 2392848384 | bytes 12563475 | solution.py:227
  15.5 13.0 %select_reduce_fusion.11 = (f32[768,384]{1,0:T(8,128)S(1)}, f32[768,384]{1,0:T(8,128)S(1)}) fusion(f32[768,8]{1,0:T(8,128)S(1)} %copy.162, s32[768,8]{1,0:T(8,128)S(1)} %copy.163, f32[768,8]{1,0:T(8,128)S(1)} %copy.164), kind=kLoop, calls=%fused_computation.17.clone.1 | loop fusion | flops 11206656 | bytes 2433024 | tf_op jit(solution)/shard_map/while/body/eval_jaxpr/reduce_sum | solution.py:129
  40.4 13.0 %select_reduce_fusion.11 = (f32[768,384]{1,0:T(8,128)S(1)}, f32[768,384]{1,0:T(8,128)S(1)}) fusion(f32[768,8]{1,0:T(8,128)S(1)} %copy.162, s32[768,8]{1,0:T(8,128)S(1)} %copy.163, f32[768,8]{1,0:T(8,128)S(1)} %copy.164), kind=kLoop, calls=%fused_computation.17.clone.1 | loop fusion | flops 11206656 | bytes 2433024 | tf_op jit(solution)/shard_map/while/body/eval_jaxpr/reduce_sum | solution.py:129
  65.4 13.0 %select_reduce_fusion.11 = (f32[768,384]{1,0:T(8,128)S(1)}, f32[768,384]{1,0:T(8,128)S(1)}) fusion(f32[768,8]{1,0:T(8,128)S(1)} %copy.162, s32[768,8]{1,0:T(8,128)S(1)} %copy.163, f32[768,8]{1,0:T(8,128)S(1)} %copy.164), kind=kLoop, calls=%fused_computation.17.clone.1 | loop fusion | flops 11206656 | bytes 2433024 | tf_op jit(solution)/shard_map/while/body/eval_jaxpr/reduce_sum | solution.py:129
  90.4 13.0 %select_reduce_fusion.11 = (f32[768,384]{1,0:T(8,128)S(1)}, f32[768,384]{1,0:T(8,128)S(1)}) fusion(f32[768,8]{1,0:T(8,128)S(1)} %copy.162, s32[768,8]{1,0:T(8,128)S(1)} %copy.163, f32[768,8]{1,0:T(8,128)S(1)} %copy.164), kind=kLoop, calls=%fused_computation.17.clone.1 | loop fusion | flops 11206656 | bytes 2433024 | tf_op jit(solution)/shard_map/while/body/eval_jaxpr/reduce_sum | solution.py:129
  151.8 23.2 %all-to-all-done = f32[4,1,75264]{2,1,0:T(1,128)S(1)} async-done(((f32[4,1,75264]{2,1,0:T(1,128)}), f32[4,1,75264]{2,1,0:T(1,128)S(1)}, u32[]{:S(2)}, u32[]{:S(2)}) %all-to-all-start) | async-done | bytes 1204256 | tf_op jit(solution)/shard_map/all_to_all | solution.py:252
  189.4 11.7 %all_to_all.55 = f32[49,2,16,192]{3,2,1,0:T(8,128)S(1)} reshape(f32[49,2,16,4,48]{4,3,2,1,0:T(4,128)} %bitcast.337) | data formatting | bytes 2408448 | tf_op jit(solution)/shard_map/all_to_all | solution.py:252
  224.2 15.1 %all-to-all-done.1 = f32[8,1,37632]{2,1,0:T(1,128)S(1)} async-done(((f32[8,1,37632]{2,1,0:T(1,128)}), f32[8,1,37632]{2,1,0:T(1,128)S(1)}, u32[]{:S(2)}, u32[]{:S(2)}) %all-to-all-start.1) | async-done | bytes 1204256 | tf_op jit(solution)/shard_map/all_to_all | solution.py:255
  274.5 19.4 %all_to_all.72 = f32[8,1,37632]{2,1,0:T(1,128)S(1)} all-to-all(f32[8,1,37632]{2,1,0:T(1,128)S(1)} %reshape.1135), channel_id=1, replica_groups=mesh['slab'=8,'pencil'=4] {'slab'}, dimensions={0} | all-to-all | bytes 2408448 | tf_op jit(solution)/shard_map/all_to_all | solution.py:275
  336.6 23.8 %all-to-all-done.3 = f32[4,1,75264]{2,1,0:T(1,128)S(1)} async-done(((f32[4,1,75264]{2,1,0:T(1,128)}), f32[4,1,75264]{2,1,0:T(1,128)S(1)}, u32[]{:S(2)}, u32[]{:S(2)}) %all-to-all-start.3) | async-done | bytes 1204256 | tf_op jit(solution)/shard_map/all_to_all | solution.py:278
  399.1 44.4 %psum.7 = f32[]{:T(128)} all-reduce(f32[]{:T(128)S(6)} %mul_shard_map.3), channel_id=1, replica_groups=mesh['slab'=8,'pencil'=4] {'slab','pencil'}, use_global_device_ids=true, to_apply=%region_17.18 | all-reduce | flops 1 | bytes 8 | tf_op jit(solution)/shard_map/psum | solution.py:272
  445.8 293.6 %while.40 = (s32[]{:T(128)}, f32[4,3,768]{2,1,0:T(4,128)S(1)}, f32[4,768,12]{1,2,0:T(8,128)}, f32[4,768,56]{1,2,0:T(8,128)}, f32[4,768,384]{2,1,0:T(8,128)}, /*i...) while((s32[]{:T(128)}, f32[4,3,768]{2,1,0:T(4,128)S(1)}, ...), condition=%wide.region_19.20_spmd, body=%wide.region_18.19_spmd.sunk | while | flops 4775567872 | bytes 50012400 | solution.py:298
  462.2 7.0 copy.169
  472.0 12.6 %fusion.369 = f32[768,1,12]{2,1,0:T(1,128)} fusion(f32[768,56,1]{1,2,0:T(1,128)S(1)} %bitcast.322, f32[768,56,12]{1,2,0:T(8,128)} %copy.169), kind=kOutput, calls=%fused_computation.446.clone.1 | convolution fusion | flops 6193152 | bytes 2273280 | tf_op jit(solution)/shard_map/while/body/eval_jaxpr/sz,sy,syz->s/dot_general | solution.py:295
  486.4 7.0 copy.167
  493.6 12.0 %fusion.368 = f32[768,1,12]{2,1,0:T(1,128)S(1)} fusion(f32[768,56,1]{1,2,0:T(1,128)S(1)} %bitcast.325, f32[768,56,12]{1,2,0:T(8,128)} %copy.167), kind=kOutput, calls=%fused_computation.445.clone.1 | convolution fusion | flops 6193152 | bytes 2273280 | tf_op jit(solution)/shard_map/while/body/eval_jaxpr/sz,sy,syz->s/dot_general | solution.py:294
  507.0 12.0 %fusion.370 = f32[768,1,12]{2,1,0:T(1,128)S(1)} fusion(f32[768,56,1]{1,2,0:T(1,128)S(1)} %bitcast.323, f32[768,56,12]{1,2,0:T(8,128)} %copy.167), kind=kOutput, calls=%fused_computation.444.clone.1 | convolution fusion | flops 6193152 | bytes 2273280 | tf_op jit(solution)/shard_map/while/body/eval_jaxpr/sz,sy,syz->s/dot_general | solution.py:293
  535.6 7.0 copy.169
  545.4 12.6 %fusion.369 = f32[768,1,12]{2,1,0:T(1,128)} fusion(f32[768,56,1]{1,2,0:T(1,128)S(1)} %bitcast.322, f32[768,56,12]{1,2,0:T(8,128)} %copy.169), kind=kOutput, calls=%fused_computation.446.clone.1 | convolution fusion | flops 6193152 | bytes 2273280 | tf_op jit(solution)/shard_map/while/body/eval_jaxpr/sz,sy,syz->s/dot_general | solution.py:295
  559.8 7.0 copy.167
  567.0 12.0 %fusion.368 = f32[768,1,12]{2,1,0:T(1,128)S(1)} fusion(f32[768,56,1]{1,2,0:T(1,128)S(1)} %bitcast.325, f32[768,56,12]{1,2,0:T(8,128)} %copy.167), kind=kOutput, calls=%fused_computation.445.clone.1 | convolution fusion | flops 6193152 | bytes 2273280 | tf_op jit(solution)/shard_map/while/body/eval_jaxpr/sz,sy,syz->s/dot_general | solution.py:294
  580.4 12.0 %fusion.370 = f32[768,1,12]{2,1,0:T(1,128)S(1)} fusion(f32[768,56,1]{1,2,0:T(1,128)S(1)} %bitcast.323, f32[768,56,12]{1,2,0:T(8,128)} %copy.167), kind=kOutput, calls=%fused_computation.444.clone.1 | convolution fusion | flops 6193152 | bytes 2273280 | tf_op jit(solution)/shard_map/while/body/eval_jaxpr/sz,sy,syz->s/dot_general | solution.py:293
  608.8 7.0 copy.169
  618.6 12.6 %fusion.369 = f32[768,1,12]{2,1,0:T(1,128)} fusion(f32[768,56,1]{1,2,0:T(1,128)S(1)} %bitcast.322, f32[768,56,12]{1,2,0:T(8,128)} %copy.169), kind=kOutput, calls=%fused_computation.446.clone.1 | convolution fusion | flops 6193152 | bytes 2273280 | tf_op jit(solution)/shard_map/while/body/eval_jaxpr/sz,sy,syz->s/dot_general | solution.py:295
  633.0 7.0 copy.167
  640.2 12.0 %fusion.368 = f32[768,1,12]{2,1,0:T(1,128)S(1)} fusion(f32[768,56,1]{1,2,0:T(1,128)S(1)} %bitcast.325, f32[768,56,12]{1,2,0:T(8,128)} %copy.167), kind=kOutput, calls=%fused_computation.445.clone.1 | convolution fusion | flops 6193152 | bytes 2273280 | tf_op jit(solution)/shard_map/while/body/eval_jaxpr/sz,sy,syz->s/dot_general | solution.py:294
  653.6 12.0 %fusion.370 = f32[768,1,12]{2,1,0:T(1,128)S(1)} fusion(f32[768,56,1]{1,2,0:T(1,128)S(1)} %bitcast.323, f32[768,56,12]{1,2,0:T(8,128)} %copy.167), kind=kOutput, calls=%fused_computation.444.clone.1 | convolution fusion | flops 6193152 | bytes 2273280 | tf_op jit(solution)/shard_map/while/body/eval_jaxpr/sz,sy,syz->s/dot_general | solution.py:293
  682.0 7.0 copy.169
  691.8 12.6 %fusion.369 = f32[768,1,12]{2,1,0:T(1,128)} fusion(f32[768,56,1]{1,2,0:T(1,128)S(1)} %bitcast.322, f32[768,56,12]{1,2,0:T(8,128)} %copy.169), kind=kOutput, calls=%fused_computation.446.clone.1 | convolution fusion | flops 6193152 | bytes 2273280 | tf_op jit(solution)/shard_map/while/body/eval_jaxpr/sz,sy,syz->s/dot_general | solution.py:295
  706.2 7.0 copy.167
  713.4 12.0 %fusion.368 = f32[768,1,12]{2,1,0:T(1,128)S(1)} fusion(f32[768,56,1]{1,2,0:T(1,128)S(1)} %bitcast.325, f32[768,56,12]{1,2,0:T(8,128)} %copy.167), kind=kOutput, calls=%fused_computation.445.clone.1 | convolution fusion | flops 6193152 | bytes 2273280 | tf_op jit(solution)/shard_map/while/body/eval_jaxpr/sz,sy,syz->s/dot_general | solution.py:294
  726.8 12.0 %fusion.370 = f32[768,1,12]{2,1,0:T(1,128)S(1)} fusion(f32[768,56,1]{1,2,0:T(1,128)S(1)} %bitcast.323, f32[768,56,12]{1,2,0:T(8,128)} %copy.167), kind=kOutput, calls=%fused_computation.444.clone.1 | convolution fusion | flops 6193152 | bytes 2273280 | tf_op jit(solution)/shard_map/while/body/eval_jaxpr/sz,sy,syz->s/dot_general | solution.py:293
  (352 shorter events, 345.6 us)
Async XLA Ops:
  2.3 4.2 copy-start.6
  31.3 7.0 copy-start.23
  38.3 1.9 copy-start.22
  56.3 7.0 copy-start.23
  63.3 1.9 copy-start.22
  81.3 7.0 copy-start.23
  88.3 1.9 copy-start.22
  106.2 7.1 copy-start.23
  113.3 5.3 copy-start.8
  114.5 10.5 %collective-permute-start = (f32[4,56,384]{2,1,0:T(8,128)S(1)}, f32[4,56,384]{2,1,0:T(8,128)S(1)}, u32[]{:S(2)}, u32[]{:S(2)}) collective-permute-start(f32[4,56,384]{2,1,0:T(8,128)S(1)} %get-tuple-element.502), channel_id=1, source_target_pairs={{0,4},{4,8},{8,12},{12,16},{16,20},{20,24},{24,28},{28,0},{1,5},{5... | collective-permute-start | bytes 1032200 | tf_op jit(solution)/shard_map/ppermute | solution.py:26
  114.6 11.5 %collective-permute-start.1 = (f32[4,56,384]{2,1,0:T(8,128)S(1)}, f32[4,56,384]{2,1,0:T(8,128)S(1)}, u32[]{:S(2)}, u32[]{:S(2)}) collective-permute-start(f32[4,56,384]{2,1,0:T(8,128)S(1)} %get-tuple-element.501), channel_id=1, source_target_pairs={{4,0},{8,4},{12,8},{16,12},{20,16},{24,20},{28,24},{0,28},{5,1},{9... | collective-permute-start | bytes 1032200 | tf_op jit(solution)/shard_map/ppermute | solution.py:28
  126.2 4.7 collective-permute-start.2
  129.2 4.9 collective-permute-start.3
  145.5 5.9 copy-start.17
  145.5 29.4 %all-to-all-start = ((f32[4,1,75264]{2,1,0:T(1,128)}), f32[4,1,75264]{2,1,0:T(1,128)S(1)}, u32[]{:S(2)}, u32[]{:S(2)}) async-start(f32[4,1,75264]{2,1,0:T(1,128)} %reshape.1131), calls=%async_computation | async-start | bytes 2408448 | tf_op jit(solution)/shard_map/all_to_all | solution.py:252
  217.9 21.4 %all-to-all-start.1 = ((f32[8,1,37632]{2,1,0:T(1,128)}), f32[8,1,37632]{2,1,0:T(1,128)S(1)}, u32[]{:S(2)}, u32[]{:S(2)}) async-start(f32[8,1,37632]{2,1,0:T(1,128)} %reshape.1133), calls=%async_computation.1 | async-start | bytes 2408448 | tf_op jit(solution)/shard_map/all_to_all | solution.py:255
  327.8 32.6 %all-to-all-start.3 = ((f32[4,1,75264]{2,1,0:T(1,128)}), f32[4,1,75264]{2,1,0:T(1,128)S(1)}, u32[]{:S(2)}, u32[]{:S(2)}) async-start(f32[4,1,75264]{2,1,0:T(1,128)} %reshape.1137), calls=%async_computation.3 | async-start | bytes 2408448 | tf_op jit(solution)/shard_map/all_to_all | solution.py:278
  377.1 4.6 copy-start.5
  385.7 13.3 %copy-start.9 = (f32[4,768]{1,0:T(4,128)S(1)}, f32[4,768]{1,0:T(4,128)}, u32[]{:S(2)}) copy-start(f32[4,768]{1,0:T(4,128)} %get-tuple-element.842) | copy-start | bytes 36868
  385.9 9.2 %collective-permute-start.4 = (f32[48,4,384]{2,1,0:T(4,128)S(1)}, f32[48,4,384]{2,1,0:T(4,128)S(1)}, u32[]{:S(2)}, u32[]{:S(2)}) collective-permute-start(f32[48,4,384]{2,1,0:T(4,128)S(1)} %get-tuple-element.509), channel_id=1, source_target_pairs={{0,4},{4,8},{8,12},{12,16},{16,20},{20,24},{24,28},{28,0},{1,5},{5... | collective-permute-start | bytes 884744 | tf_op jit(solution)/shard_map/ppermute | solution.py:26
  385.9 9.1 %collective-permute-start.5 = (f32[48,4,384]{2,1,0:T(4,128)S(1)}, f32[48,4,384]{2,1,0:T(4,128)S(1)}, u32[]{:S(2)}, u32[]{:S(2)}) collective-permute-start(f32[48,4,384]{2,1,0:T(4,128)S(1)} %get-tuple-element.510), channel_id=1, source_target_pairs={{4,0},{8,4},{12,8},{16,12},{20,16},{24,20},{28,24},{0,28},{5,1},{9... | collective-permute-start | bytes 884744 | tf_op jit(solution)/shard_map/ppermute | solution.py:28
  395.1 49.1 %collective-permute-start.6 = (f32[4,24,384]{2,1,0:T(8,128)S(1)}, f32[4,24,384]{2,1,0:T(8,128)S(1)}, u32[]{:S(2)}, u32[]{:S(2)}) collective-permute-start(f32[4,24,384]{2,1,0:T(8,128)S(1)} %get-tuple-element.503), channel_id=1, source_target_pairs={{0,1},{1,2},{2,3},{3,0},{4,5},{5,6},{6,7},{7,4},{8,9},{9,10},{10,1... | collective-permute-start | bytes 442376 | tf_op jit(solution)/shard_map/ppermute | solution.py:26
  396.6 47.6 %collective-permute-start.7 = (f32[4,24,384]{2,1,0:T(8,128)S(1)}, f32[4,24,384]{2,1,0:T(8,128)S(1)}, u32[]{:S(2)}, u32[]{:S(2)}) collective-permute-start(f32[4,24,384]{2,1,0:T(8,128)S(1)} %get-tuple-element.504), channel_id=1, source_target_pairs={{1,0},{2,1},{3,2},{0,3},{5,4},{6,5},{7,6},{4,7},{9,8},{10,9},{11,1... | collective-permute-start | bytes 442376 | tf_op jit(solution)/shard_map/ppermute | solution.py:28
  445.8 293.8 %copy-start.10 = (f32[1536,3]{0,1:T(4,128)S(1)}, f32[1536,3]{0,1:T(4,128)}, u32[]{:S(2)}) copy-start(f32[1536,3]{0,1:T(4,128)} %get-tuple-element.522) | copy-start | bytes 55300
  445.8 293.8 %copy-start.15 = (bf16[3,256]{1,0:T(4,128)(2,1)S(1)}, bf16[3,256]{1,0:T(4,128)(2,1)}, u32[]{:S(2)}) copy-start(bf16[3,256]{1,0:T(4,128)(2,1)} %param.37) | copy-start | bytes 4612
  493.6 13.1 %copy-start.1 = (f32[768,1,12]{2,1,0:T(1,128)S(1)}, f32[768,1,12]{2,1,0:T(1,128)}, u32[]{:S(2)}) copy-start(f32[768,1,12]{2,1,0:T(1,128)} %fusion.369) | copy-start | bytes 110596 | tf_op jit(solution)/shard_map/while
  567.0 13.1 %copy-start.1 = (f32[768,1,12]{2,1,0:T(1,128)S(1)}, f32[768,1,12]{2,1,0:T(1,128)}, u32[]{:S(2)}) copy-start(f32[768,1,12]{2,1,0:T(1,128)} %fusion.369) | copy-start | bytes 110596 | tf_op jit(solution)/shard_map/while
  640.2 13.1 %copy-start.1 = (f32[768,1,12]{2,1,0:T(1,128)S(1)}, f32[768,1,12]{2,1,0:T(1,128)}, u32[]{:S(2)}) copy-start(f32[768,1,12]{2,1,0:T(1,128)} %fusion.369) | copy-start | bytes 110596 | tf_op jit(solution)/shard_map/while
  713.4 13.1 %copy-start.1 = (f32[768,1,12]{2,1,0:T(1,128)S(1)}, f32[768,1,12]{2,1,0:T(1,128)}, u32[]{:S(2)}) copy-start(f32[768,1,12]{2,1,0:T(1,128)} %fusion.369) | copy-start | bytes 110596 | tf_op jit(solution)/shard_map/while
  739.5 2.6 copy-start.12
  740.1 2.1 copy-start.4
  740.1 2.1 copy-start.7
  (12 other events, 17.9 us)
where the time goes:
time: 760 us; the launch traced here: 749 us
  matrix products  254 us (33%)
  local copies, waits for them, and re-layouts  231 us (30%)
  other arithmetic  79.9 us (11%)
  waiting for transfers between devices  79 us (10%)
  blocking collectives  63.9 us (8%)
  starting transfers between devices  29.8 us (4%)
    reduce_sum x12, other arithmetic, dense_window(): jnp.sum(jnp.where(matches, spline_slope[:, :, None], 0.0), axis=1)  53.9 us
    dot_general x4, matrix products, sample_step(): jnp.einsum('sz,sy,syz->s', plane_val, row_val, across, precision=highest)  50.6 us
    dot_general x4, matrix products, sample_step(): jnp.einsum('sz,sy,syz->s', plane_val, row_slope, along, precision=highest)  48.1 us
    dot_general x4, matrix products, sample_step(): jnp.einsum('sz,sy,syz->s', plane_slope, row_val, along, precision=highest)  47.9 us
    unnamed x52, local copies, waits for them, and re-layouts  45 us
    psum x1, blocking collectives, body(): energy_sum = lax.psum(energy_terms, ('slab', 'pencil'))  44.4 us
    reshape x8, local copies, waits for them, and re-layouts, sample_step(): across = both[site_count:].reshape(site_count, CY + 8, BZ + 8)  40.4 us
    dot_general x17, matrix products, lead_product(): lax.dot_general(table, data, (((1,), (dim,)), ((), ())), precision=highest)  39.6 us
  transfers between devices with their start and end apart: 11, of which 7 were waited for; matrix products, arithmetic and copies ran while one was open for 1% of the time, Pallas kernels for 0%

commit v1 on v0

--- a/solution.py
+++ b/solution.py
@@ -14,6 +14,29 @@
 ewald_beta = 1.4
 shift_scale = 0.9
 highest = lax.Precision.HIGHEST
+
+
+def in_blocks(x, dim, size):
+    lengths = x.shape
+    tiles = x.reshape(*lengths[:dim], size, lengths[dim] // size, *lengths[dim + 1 :])
+    return jnp.moveaxis(tiles, dim, 0)
+
+
+def joined_along(pieces, dim):
+    pieces = jnp.moveaxis(pieces, 0, dim)
+    shape = pieces.shape
+    return pieces.reshape(*shape[:dim], shape[dim] * shape[dim + 1], *shape[dim + 2 :])
+
+
+def pairwise_exchange(shard, axis, split_dim, concat_dim):
+    size, position = (lax.axis_size(axis), lax.axis_index(axis))
+    pieces = in_blocks(shard, split_dim, size)
+    finished = [pieces[position]]
+    for step in range(1, size):
+        sent = pieces[position ^ step]
+        finished.append(lax.ppermute(sent, axis, [(i, i ^ step) for i in range(size)]))
+    pieces = jnp.stack(finished)[position ^ jnp.arange(size)]
+    return joined_along(pieces, concat_dim)
 
 
 def extended(cells, sides, width):
@@ -249,7 +272,7 @@
     spectrum = lead_product(forward_rows, source_grid, 2).reshape(
         wave_cols, 2, plane_here, row_here
     )
-    spectrum = lax.all_to_all(spectrum, "pencil", split_axis=0, concat_axis=3, tiled=True)
+    spectrum = pairwise_exchange(spectrum, "pencil", 0, 3)
     real_y, imag_y = forward_pair(row_cos, row_sin, spectrum[:, 0], spectrum[:, 1], 2)
     spectrum = jnp.stack([real_y, imag_y], axis=1)
     spectrum = lax.all_to_all(spectrum, "slab", split_axis=0, concat_axis=3, tiled=True)

time: 760 us -> 778 us (1.024)
  waiting for transfers between devices: 79 us -> 113 us
  local copies, waits for them, and re-layouts: 231 us -> 215 us
    ppermute x0 -> x3, waiting for transfers between devices: none -> 66 us  [pairwise_exchange(): lax.ppermute(sent, axis, [(i, i ^ step) for i in range(size)])]
    all_to_all x1 -> x0, waiting for transfers between devices: 23.2 us -> none  [body(): lax.all_to_all(spectrum, 'pencil', split_axis=0, concat_axis=3, tiled=True)]
    all_to_all x3 -> x0, local copies, waits for them, and re-layouts: 18.8 us -> none  [body(): lax.all_to_all(spectrum, 'pencil', split_axis=0, concat_axis=3, tiled=True)]
    unnamed x52 -> x50, local copies, waits for them, and re-layouts: 45 us -> 36.4 us
    all_to_all x1, waiting for transfers between devices: 15.1 us -> 6.77 us  [body(): lax.all_to_all(spectrum, 'slab', split_axis=0, concat_axis=3, tiled=True)]
    reshape x0 -> x2, local copies, waits for them, and re-layouts: none -> 8.27 us  [joined_along(): pieces.reshape(*shape[:dim], shape[dim] * shape[dim + 1], *shape[dim + 2:])]
    all_to_all x1, starting transfers between devices: 6.01 us -> 14.2 us  [body(): lax.all_to_all(spectrum, 'slab', split_axis=0, concat_axis=3, tiled=True)]
  transfers between devices with their start and end apart: 11 -> 13, of which waited for: 7 -> 9; matrix products, arithmetic and copies ran while one was open for 1% -> 1% of each run, Pallas kernels for 0% -> 0%
where the time goes in v1:
time: 778 us; the launch traced here: 767 us
  matrix products  255 us (33%)
  local copies, waits for them, and re-layouts  215 us (28%)
  waiting for transfers between devices  113 us (15%)
  other arithmetic  77.9 us (10%)
  blocking collectives  63.9 us (8%)
  starting transfers between devices  31.6 us (4%)
    ppermute x3, waiting for transfers between devices, pairwise_exchange(): lax.ppermute(sent, axis, [(i, i ^ step) for i in range(size)])  66 us
    reduce_sum x12, other arithmetic, dense_window(): jnp.sum(jnp.where(matches, spline_slope[:, :, None], 0.0), axis=1)  53.9 us
    dot_general x4, matrix products, sample_step(): jnp.einsum('sz,sy,syz->s', plane_val, row_val, across, precision=highest)  50.6 us
    dot_general x4, matrix products, sample_step(): jnp.einsum('sz,sy,syz->s', plane_val, row_slope, along, precision=highest)  48.1 us
    dot_general x4, matrix products, sample_step(): jnp.einsum('sz,sy,syz->s', plane_slope, row_val, along, precision=highest)  47.9 us
    psum x1, blocking collectives, body(): energy_sum = lax.psum(energy_terms, ('slab', 'pencil'))  44.4 us
    dot_general x17, matrix products, lead_product(): lax.dot_general(table, data, (((1,), (dim,)), ((), ())), precision=highest)  40.8 us
    reshape x8, local copies, waits for them, and re-layouts, sample_step(): across = both[site_count:].reshape(site_count, CY + 8, BZ + 8)  40.4 us
  transfers between devices with their start and end apart: 13, of which 9 were waited for; matrix products, arithmetic and copies ran while one was open for 1% of the time, Pallas kernels for 0%

profile of v1, /device:TPU:12, one launch (start us, length us, event | category | flops | bytes accessed | tf_op | source)
XLA Modules:
  0.0 767.3 jit_solution(7986830021628021637)
XLA Ops:
  13.4 99.9 %while.39 = (s32[]{:T(128)}, f32[24,56,384]{2,1,0:T(8,128)}, f32[4,768,12]{1,2,0:T(8,128)S(1)}, f32[4,768,12]{1,2,0:T(8,128)}, f32[4,768,56]{1,2,0:T(8,128)}, /*...) while((s32[]{:T(128)}, f32[24,56,384]{2,1,0:T(8,128)}, ...), condition=%wide.region_9.10_spmd, body=%wide.region_2.9_spmd.sunk | while | flops 2392848384 | bytes 12563475 | solution.py:250
  15.5 13.0 %select_reduce_fusion.11 = (f32[768,384]{1,0:T(8,128)S(1)}, f32[768,384]{1,0:T(8,128)S(1)}) fusion(f32[768,8]{1,0:T(8,128)S(1)} %copy.152, s32[768,8]{1,0:T(8,128)S(1)} %copy.153, f32[768,8]{1,0:T(8,128)S(1)} %copy.154), kind=kLoop, calls=%fused_computation.18.clone.1 | loop fusion | flops 11206656 | bytes 2433024 | tf_op jit(solution)/shard_map/while/body/eval_jaxpr/reduce_sum | solution.py:152
  40.4 13.0 %select_reduce_fusion.11 = (f32[768,384]{1,0:T(8,128)S(1)}, f32[768,384]{1,0:T(8,128)S(1)}) fusion(f32[768,8]{1,0:T(8,128)S(1)} %copy.152, s32[768,8]{1,0:T(8,128)S(1)} %copy.153, f32[768,8]{1,0:T(8,128)S(1)} %copy.154), kind=kLoop, calls=%fused_computation.18.clone.1 | loop fusion | flops 11206656 | bytes 2433024 | tf_op jit(solution)/shard_map/while/body/eval_jaxpr/reduce_sum | solution.py:152
  65.4 13.0 %select_reduce_fusion.11 = (f32[768,384]{1,0:T(8,128)S(1)}, f32[768,384]{1,0:T(8,128)S(1)}) fusion(f32[768,8]{1,0:T(8,128)S(1)} %copy.152, s32[768,8]{1,0:T(8,128)S(1)} %copy.153, f32[768,8]{1,0:T(8,128)S(1)} %copy.154), kind=kLoop, calls=%fused_computation.18.clone.1 | loop fusion | flops 11206656 | bytes 2433024 | tf_op jit(solution)/shard_map/while/body/eval_jaxpr/reduce_sum | solution.py:152
  90.4 13.0 %select_reduce_fusion.11 = (f32[768,384]{1,0:T(8,128)S(1)}, f32[768,384]{1,0:T(8,128)S(1)}) fusion(f32[768,8]{1,0:T(8,128)S(1)} %copy.152, s32[768,8]{1,0:T(8,128)S(1)} %copy.153, f32[768,8]{1,0:T(8,128)S(1)} %copy.154), kind=kLoop, calls=%fused_computation.18.clone.1 | loop fusion | flops 11206656 | bytes 2433024 | tf_op jit(solution)/shard_map/while/body/eval_jaxpr/reduce_sum | solution.py:152
  143.5 27.1 %collective-permute-done.4 = f32[49,2,16,48]{0,3,2,1:T(8,128)S(1)} collective-permute-done((f32[49,2,16,48]{0,3,2,1:T(8,128)S(1)}, f32[49,2,16,48]{0,3,2,1:T(8,128)S(1)}, u32[]{:S(2)}, u32[]{:S(2)}) %collective-permute-start.4) | collective-permute-done | bytes 301088 | tf_op jit(solution)/shard_map/ppermute | solution.py:37
  170.6 23.8 %collective-permute-done.5 = f32[49,2,16,48]{0,3,2,1:T(8,128)S(1)} collective-permute-done((f32[49,2,16,48]{0,3,2,1:T(8,128)S(1)}, f32[49,2,16,48]{0,3,2,1:T(8,128)S(1)}, u32[]{:S(2)}, u32[]{:S(2)}) %collective-permute-start.5) | collective-permute-done | bytes 301088 | tf_op jit(solution)/shard_map/ppermute | solution.py:37
  194.5 15.1 %collective-permute-done.6 = f32[49,2,16,48]{0,3,2,1:T(8,128)S(1)} collective-permute-done((f32[49,2,16,48]{0,3,2,1:T(8,128)S(1)}, f32[49,2,16,48]{0,3,2,1:T(8,128)S(1)}, u32[]{:S(2)}, u32[]{:S(2)}) %collective-permute-start.6) | collective-permute-done | bytes 301088 | tf_op jit(solution)/shard_map/ppermute | solution.py:37
  239.7 14.2 %all-to-all-start = ((f32[8,1,37632]{2,1,0:T(1,128)}), f32[8,1,37632]{2,1,0:T(1,128)S(1)}, u32[]{:S(2)}, u32[]{:S(2)}) async-start(f32[8,1,37632]{2,1,0:T(1,128)} %reshape.1154), calls=%async_computation | async-start | bytes 2408448 | tf_op jit(solution)/shard_map/all_to_all | solution.py:278
  296.6 19.5 %all_to_all.54 = f32[8,1,37632]{2,1,0:T(1,128)S(1)} all-to-all(f32[8,1,37632]{2,1,0:T(1,128)S(1)} %reshape.1156), channel_id=1, replica_groups=mesh['slab'=8,'pencil'=4] {'slab'}, dimensions={0} | all-to-all | bytes 2408448 | tf_op jit(solution)/shard_map/all_to_all | solution.py:298
  355.4 24.1 %all-to-all-done.2 = f32[4,1,75264]{2,1,0:T(1,128)S(1)} async-done(((f32[4,1,75264]{2,1,0:T(1,128)}), f32[4,1,75264]{2,1,0:T(1,128)S(1)}, u32[]{:S(2)}, u32[]{:S(2)}) %all-to-all-start.2) | async-done | bytes 1204256 | tf_op jit(solution)/shard_map/all_to_all | solution.py:301
  417.2 44.4 %psum.7 = f32[]{:T(128)} all-reduce(f32[]{:T(128)S(6)} %mul_shard_map.3), channel_id=1, replica_groups=mesh['slab'=8,'pencil'=4] {'slab','pencil'}, use_global_device_ids=true, to_apply=%region_17.18 | all-reduce | flops 1 | bytes 8 | tf_op jit(solution)/shard_map/psum | solution.py:295
  463.9 293.6 %while.40 = (s32[]{:T(128)}, f32[4,3,768]{2,1,0:T(4,128)S(1)}, f32[4,768,12]{1,2,0:T(8,128)}, f32[4,768,56]{1,2,0:T(8,128)}, f32[4,768,384]{2,1,0:T(8,128)}, /*i...) while((s32[]{:T(128)}, f32[4,3,768]{2,1,0:T(4,128)S(1)}, ...), condition=%wide.region_19.20_spmd, body=%wide.region_18.19_spmd.sunk | while | flops 4775567872 | bytes 50012400 | solution.py:321
  480.3 7.0 copy.159
  490.1 12.6 %fusion.370 = f32[768,1,12]{2,1,0:T(1,128)} fusion(f32[768,56,1]{1,2,0:T(1,128)S(1)} %bitcast.334, f32[768,56,12]{1,2,0:T(8,128)} %copy.159), kind=kOutput, calls=%fused_computation.456.clone.1 | convolution fusion | flops 6193152 | bytes 2273280 | tf_op jit(solution)/shard_map/while/body/eval_jaxpr/sz,sy,syz->s/dot_general | solution.py:318
  504.5 7.0 copy.157
  511.7 12.0 %fusion.369 = f32[768,1,12]{2,1,0:T(1,128)S(1)} fusion(f32[768,56,1]{1,2,0:T(1,128)S(1)} %bitcast.337, f32[768,56,12]{1,2,0:T(8,128)} %copy.157), kind=kOutput, calls=%fused_computation.455.clone.1 | convolution fusion | flops 6193152 | bytes 2273280 | tf_op jit(solution)/shard_map/while/body/eval_jaxpr/sz,sy,syz->s/dot_general | solution.py:317
  525.1 12.0 %fusion.371 = f32[768,1,12]{2,1,0:T(1,128)S(1)} fusion(f32[768,56,1]{1,2,0:T(1,128)S(1)} %bitcast.335, f32[768,56,12]{1,2,0:T(8,128)} %copy.157), kind=kOutput, calls=%fused_computation.454.clone.1 | convolution fusion | flops 6193152 | bytes 2273280 | tf_op jit(solution)/shard_map/while/body/eval_jaxpr/sz,sy,syz->s/dot_general | solution.py:316
  553.7 7.0 copy.159
  563.6 12.6 %fusion.370 = f32[768,1,12]{2,1,0:T(1,128)} fusion(f32[768,56,1]{1,2,0:T(1,128)S(1)} %bitcast.334, f32[768,56,12]{1,2,0:T(8,128)} %copy.159), kind=kOutput, calls=%fused_computation.456.clone.1 | convolution fusion | flops 6193152 | bytes 2273280 | tf_op jit(solution)/shard_map/while/body/eval_jaxpr/sz,sy,syz->s/dot_general | solution.py:318
  577.9 7.0 copy.157
  585.2 12.0 %fusion.369 = f32[768,1,12]{2,1,0:T(1,128)S(1)} fusion(f32[768,56,1]{1,2,0:T(1,128)S(1)} %bitcast.337, f32[768,56,12]{1,2,0:T(8,128)} %copy.157), kind=kOutput, calls=%fused_computation.455.clone.1 | convolution fusion | flops 6193152 | bytes 2273280 | tf_op jit(solution)/shard_map/while/body/eval_jaxpr/sz,sy,syz->s/dot_general | solution.py:317
  598.5 12.0 %fusion.371 = f32[768,1,12]{2,1,0:T(1,128)S(1)} fusion(f32[768,56,1]{1,2,0:T(1,128)S(1)} %bitcast.335, f32[768,56,12]{1,2,0:T(8,128)} %copy.157), kind=kOutput, calls=%fused_computation.454.clone.1 | convolution fusion | flops 6193152 | bytes 2273280 | tf_op jit(solution)/shard_map/while/body/eval_jaxpr/sz,sy,syz->s/dot_general | solution.py:316
  627.0 7.0 copy.159
  636.8 12.6 %fusion.370 = f32[768,1,12]{2,1,0:T(1,128)} fusion(f32[768,56,1]{1,2,0:T(1,128)S(1)} %bitcast.334, f32[768,56,12]{1,2,0:T(8,128)} %copy.159), kind=kOutput, calls=%fused_computation.456.clone.1 | convolution fusion | flops 6193152 | bytes 2273280 | tf_op jit(solution)/shard_map/while/body/eval_jaxpr/sz,sy,syz->s/dot_general | solution.py:318
  651.2 7.0 copy.157
  658.4 12.0 %fusion.369 = f32[768,1,12]{2,1,0:T(1,128)S(1)} fusion(f32[768,56,1]{1,2,0:T(1,128)S(1)} %bitcast.337, f32[768,56,12]{1,2,0:T(8,128)} %copy.157), kind=kOutput, calls=%fused_computation.455.clone.1 | convolution fusion | flops 6193152 | bytes 2273280 | tf_op jit(solution)/shard_map/while/body/eval_jaxpr/sz,sy,syz->s/dot_general | solution.py:317
  671.7 12.0 %fusion.371 = f32[768,1,12]{2,1,0:T(1,128)S(1)} fusion(f32[768,56,1]{1,2,0:T(1,128)S(1)} %bitcast.335, f32[768,56,12]{1,2,0:T(8,128)} %copy.157), kind=kOutput, calls=%fused_computation.454.clone.1 | convolution fusion | flops 6193152 | bytes 2273280 | tf_op jit(solution)/shard_map/while/body/eval_jaxpr/sz,sy,syz->s/dot_general | solution.py:316
  710.0 12.6 %fusion.370 = f32[768,1,12]{2,1,0:T(1,128)} fusion(f32[768,56,1]{1,2,0:T(1,128)S(1)} %bitcast.334, f32[768,56,12]{1,2,0:T(8,128)} %copy.159), kind=kOutput, calls=%fused_computation.456.clone.1 | convolution fusion | flops 6193152 | bytes 2273280 | tf_op jit(solution)/shard_map/while/body/eval_jaxpr/sz,sy,syz->s/dot_general | solution.py:318
  724.4 7.0 copy.157
  731.6 12.0 %fusion.369 = f32[768,1,12]{2,1,0:T(1,128)S(1)} fusion(f32[768,56,1]{1,2,0:T(1,128)S(1)} %bitcast.337, f32[768,56,12]{1,2,0:T(8,128)} %copy.157), kind=kOutput, calls=%fused_computation.455.clone.1 | convolution fusion | flops 6193152 | bytes 2273280 | tf_op jit(solution)/shard_map/while/body/eval_jaxpr/sz,sy,syz->s/dot_general | solution.py:317
  744.9 12.0 %fusion.371 = f32[768,1,12]{2,1,0:T(1,128)S(1)} fusion(f32[768,56,1]{1,2,0:T(1,128)S(1)} %bitcast.335, f32[768,56,12]{1,2,0:T(8,128)} %copy.157), kind=kOutput, calls=%fused_computation.454.clone.1 | convolution fusion | flops 6193152 | bytes 2273280 | tf_op jit(solution)/shard_map/while/body/eval_jaxpr/sz,sy,syz->s/dot_general | solution.py:316
  (358 shorter events, 340.1 us)
Async XLA Ops:
  2.3 4.2 copy-start.6
  31.3 7.0 copy-start.23
  38.3 1.9 copy-start.22
  56.3 7.0 copy-start.23
  81.3 7.0 copy-start.23
  106.2 7.1 copy-start.23
  113.3 6.1 copy-start.8
  113.3 6.1 copy-start.17
  115.3 10.9 %collective-permute-start = (f32[4,56,384]{2,1,0:T(8,128)}, f32[4,56,384]{2,1,0:T(8,128)S(1)}, u32[]{:S(2)}, u32[]{:S(2)}) collective-permute-start(f32[4,56,384]{2,1,0:T(8,128)} %get-tuple-element.506), channel_id=1, source_target_pairs={{0,4},{4,8},{8,12},{12,16},{16,20},{20,24},{24,28},{28,0},{1,5},{5... | collective-permute-start | bytes 1032200 | tf_op jit(solution)/shard_map/ppermute | solution.py:49
  115.3 11.9 %collective-permute-start.1 = (f32[4,56,384]{2,1,0:T(8,128)S(1)}, f32[4,56,384]{2,1,0:T(8,128)S(1)}, u32[]{:S(2)}, u32[]{:S(2)}) collective-permute-start(f32[4,56,384]{2,1,0:T(8,128)S(1)} %get-tuple-element.505), channel_id=1, source_target_pairs={{4,0},{8,4},{12,8},{16,12},{20,16},{24,20},{28,24},{0,28},{5,1},{9... | collective-permute-start | bytes 1032200 | tf_op jit(solution)/shard_map/ppermute | solution.py:51
  127.3 5.5 collective-permute-start.2
  129.1 5.3 collective-permute-start.3
  140.0 30.7 %collective-permute-start.4 = (f32[49,2,16,48]{0,3,2,1:T(8,128)S(1)}, f32[49,2,16,48]{0,3,2,1:T(8,128)S(1)}, u32[]{:S(2)}, u32[]{:S(2)}) collective-permute-start(f32[49,2,16,48]{0,3,2,1:T(8,128)S(1)} %get-tuple-element.504), channel_id=1, source_target_pairs={{0,1},{1,0},{2,3},{3,2},{4,5},{5,4},{6,7},{7,6},{8,9},{9,8},{10,11... | collective-permute-start | bytes 903176 | tf_op jit(solution)/shard_map/ppermute | solution.py:37
  141.0 53.5 %collective-permute-start.5 = (f32[49,2,16,48]{0,3,2,1:T(8,128)S(1)}, f32[49,2,16,48]{0,3,2,1:T(8,128)S(1)}, u32[]{:S(2)}, u32[]{:S(2)}) collective-permute-start(f32[49,2,16,48]{0,3,2,1:T(8,128)S(1)} %get-tuple-element.503), channel_id=1, source_target_pairs={{0,2},{1,3},{2,0},{3,1},{4,6},{5,7},{6,4},{7,5},{8,10},{9,11},{10,... | collective-permute-start | bytes 903176 | tf_op jit(solution)/shard_map/ppermute | solution.py:37
  142.8 66.8 %collective-permute-start.6 = (f32[49,2,16,48]{0,3,2,1:T(8,128)S(1)}, f32[49,2,16,48]{0,3,2,1:T(8,128)S(1)}, u32[]{:S(2)}, u32[]{:S(2)}) collective-permute-start(f32[49,2,16,48]{0,3,2,1:T(8,128)S(1)} %get-tuple-element.502), channel_id=1, source_target_pairs={{0,3},{1,2},{2,1},{3,0},{4,7},{5,6},{6,5},{7,4},{8,11},{9,10},{10,... | collective-permute-start | bytes 903176 | tf_op jit(solution)/shard_map/ppermute | solution.py:37
  239.7 21.3 %all-to-all-start = ((f32[8,1,37632]{2,1,0:T(1,128)}), f32[8,1,37632]{2,1,0:T(1,128)S(1)}, u32[]{:S(2)}, u32[]{:S(2)}) async-start(f32[8,1,37632]{2,1,0:T(1,128)} %reshape.1154), calls=%async_computation | async-start | bytes 2408448 | tf_op jit(solution)/shard_map/all_to_all | solution.py:278
  349.8 29.7 %all-to-all-start.2 = ((f32[4,1,75264]{2,1,0:T(1,128)}), f32[4,1,75264]{2,1,0:T(1,128)S(1)}, u32[]{:S(2)}, u32[]{:S(2)}) async-start(f32[4,1,75264]{2,1,0:T(1,128)} %reshape.1158), calls=%async_computation.2 | async-start | bytes 2408448 | tf_op jit(solution)/shard_map/all_to_all | solution.py:301
  396.1 4.5 copy-start.5
  404.7 12.5 %copy-start.9 = (f32[4,768]{1,0:T(4,128)S(1)}, f32[4,768]{1,0:T(4,128)}, u32[]{:S(2)}) copy-start(f32[4,768]{1,0:T(4,128)} %get-tuple-element.848) | copy-start | bytes 36868
  404.8 9.2 %collective-permute-start.7 = (f32[48,4,384]{2,1,0:T(4,128)S(1)}, f32[48,4,384]{2,1,0:T(4,128)S(1)}, u32[]{:S(2)}, u32[]{:S(2)}) collective-permute-start(f32[48,4,384]{2,1,0:T(4,128)S(1)} %get-tuple-element.511), channel_id=1, source_target_pairs={{0,4},{4,8},{8,12},{12,16},{16,20},{20,24},{24,28},{28,0},{1,5},{5... | collective-permute-start | bytes 884744 | tf_op jit(solution)/shard_map/ppermute | solution.py:49
  404.9 9.1 %collective-permute-start.8 = (f32[48,4,384]{2,1,0:T(4,128)S(1)}, f32[48,4,384]{2,1,0:T(4,128)S(1)}, u32[]{:S(2)}, u32[]{:S(2)}) collective-permute-start(f32[48,4,384]{2,1,0:T(4,128)S(1)} %get-tuple-element.512), channel_id=1, source_target_pairs={{4,0},{8,4},{12,8},{16,12},{20,16},{24,20},{28,24},{0,28},{5,1},{9... | collective-permute-start | bytes 884744 | tf_op jit(solution)/shard_map/ppermute | solution.py:51
  414.0 48.3 %collective-permute-start.10 = (f32[4,24,384]{2,1,0:T(8,128)S(1)}, f32[4,24,384]{2,1,0:T(8,128)S(1)}, u32[]{:S(2)}, u32[]{:S(2)}) collective-permute-start(f32[4,24,384]{2,1,0:T(8,128)S(1)} %get-tuple-element.508), channel_id=1, source_target_pairs={{1,0},{2,1},{3,2},{0,3},{5,4},{6,5},{7,6},{4,7},{9,8},{10,9},{11,1... | collective-permute-start | bytes 442376 | tf_op jit(solution)/shard_map/ppermute | solution.py:51
  416.6 45.7 %collective-permute-start.9 = (f32[4,24,384]{2,1,0:T(8,128)S(1)}, f32[4,24,384]{2,1,0:T(8,128)S(1)}, u32[]{:S(2)}, u32[]{:S(2)}) collective-permute-start(f32[4,24,384]{2,1,0:T(8,128)S(1)} %get-tuple-element.507), channel_id=1, source_target_pairs={{0,1},{1,2},{2,3},{3,0},{4,5},{5,6},{6,7},{7,4},{8,9},{9,10},{10,1... | collective-permute-start | bytes 442376 | tf_op jit(solution)/shard_map/ppermute | solution.py:49
  463.9 293.8 %copy-start.10 = (f32[1536,3]{0,1:T(4,128)S(1)}, f32[1536,3]{0,1:T(4,128)}, u32[]{:S(2)}) copy-start(f32[1536,3]{0,1:T(4,128)} %get-tuple-element.524) | copy-start | bytes 55300
  463.9 293.8 %copy-start.15 = (bf16[3,256]{1,0:T(4,128)(2,1)S(1)}, bf16[3,256]{1,0:T(4,128)(2,1)}, u32[]{:S(2)}) copy-start(bf16[3,256]{1,0:T(4,128)(2,1)} %param.37) | copy-start | bytes 4612
  511.7 13.1 %copy-start.1 = (f32[768,1,12]{2,1,0:T(1,128)S(1)}, f32[768,1,12]{2,1,0:T(1,128)}, u32[]{:S(2)}) copy-start(f32[768,1,12]{2,1,0:T(1,128)} %fusion.370) | copy-start | bytes 110596 | tf_op jit(solution)/shard_map/while
  585.1 13.1 %copy-start.1 = (f32[768,1,12]{2,1,0:T(1,128)S(1)}, f32[768,1,12]{2,1,0:T(1,128)}, u32[]{:S(2)}) copy-start(f32[768,1,12]{2,1,0:T(1,128)} %fusion.370) | copy-start | bytes 110596 | tf_op jit(solution)/shard_map/while
  658.4 13.1 %copy-start.1 = (f32[768,1,12]{2,1,0:T(1,128)S(1)}, f32[768,1,12]{2,1,0:T(1,128)}, u32[]{:S(2)}) copy-start(f32[768,1,12]{2,1,0:T(1,128)} %fusion.370) | copy-start | bytes 110596 | tf_op jit(solution)/shard_map/while
  731.6 13.1 %copy-start.1 = (f32[768,1,12]{2,1,0:T(1,128)S(1)}, f32[768,1,12]{2,1,0:T(1,128)}, u32[]{:S(2)}) copy-start(f32[768,1,12]{2,1,0:T(1,128)} %fusion.370) | copy-start | bytes 110596 | tf_op jit(solution)/shard_map/while
  757.6 2.6 copy-start.12
  758.2 2.1 copy-start.4
  758.2 2.1 copy-start.7
  (14 other events, 21.6 us)
